TPU v7x, 256 devices: a whole 4x4x8 slice. The times are simulated.
256 devices in a mesh: batch: 16 (over y_hi, z), gx: 4 (over y_lo, core), gy: 4 (over x).
Axes of the slice: x: 4, y: 4 (y_hi: 2, y_lo: 2; y = y_hi * 2 + y_lo), z: 8, core: 2. Of those that a mesh axis runs over, the one named last changes fastest.
Arguments:
- features: bfloat16 [1024, 64, 4, 256], P(('batch', 'gx'), 'gy'), parts along dimension 0, may hold values from -6 to 6
- conv_weight: bfloat16 [6912, 256], replicated, may hold values from -0.078125 to 0.078125
- down_weight: bfloat16 [2048, 512], replicated, may hold values from -0.125 to 0.125
- norm_gain: float32 [512], replicated, may hold values from 0.1 to 1.9
- qkv_weight: bfloat16 [512, 1536], replicated, may hold values from -0.25 to 0.25
- out_weight: bfloat16 [512, 512], replicated, may hold values from -0.25 to 0.25
- upstream: bfloat16 [512, 32, 2, 512], P(('batch', 'gx'), 'gy'), parts along dimension 0, may hold values from -6 to 6
Outputs:
- grad_features: bfloat16 [1024, 64, 4, 256], P(('batch', 'gx'), 'gy'), parts along dimension 0
- grad_conv: bfloat16 [110592, 256], P(('batch', 'gx', 'gy')), parts along dimension 0
- grad_down: bfloat16 [32768, 512], P(('batch', 'gx', 'gy')), parts along dimension 0
- grad_gain: float32 [8192], P(('batch', 'gx', 'gy')), parts along dimension 0
- grad_qkv: bfloat16 [8192, 1536], P(('batch', 'gx', 'gy')), parts along dimension 0
- grad_out: bfloat16 [8192, 512], P(('batch', 'gx', 'gy')), parts along dimension 0
There are 16 independent parts, one for each index of `batch`. A program takes and returns all parts, laid end to end along the dimension named above; an argument that names none is the same for every part. Nothing has to cross between parts.
All inputs are finite; a program needn't handle non-finite values.
Results may differ from a plain program's by a relative error of at most 0.02.
Values may be sent and summed in bfloat16 or wider, within the bound.
No kernel may reach another device: no remote copies, remote signals or barrier semaphores. Data moves between devices by JAX's collectives and lax.ppermute only.
A program may use at most 128 MiB of HBM per device.

v0:
```python
import jax
import jax.numpy as jnp
from jax import lax
from jax.sharding import PartitionSpec as P

H = 8
HD = 64
precise = lax.Precision.HIGHEST


def padded_2(block, sides, width):
    for axis, dim in sides:
        count = lax.axis_size(axis)
        forward = [(i, i + 1) for i in range(count - 1)]
        backward = [(target, source) for source, target in forward]
        low = lax.ppermute(
            lax.slice_in_dim(block, block.shape[dim] - width, None, axis=dim), axis, forward
        )
        high = lax.ppermute(lax.slice_in_dim(block, 0, width, axis=dim), axis, backward)
        block = jnp.concatenate([low, block, high], axis=dim)
    return block


def to_tokens(volume):
    extent_x, extent_y, extent_z, channels = volume.shape
    grid = volume.reshape(extent_x // 2, 2, extent_y // 2, 2, extent_z // 2, 2, channels)
    grid = grid.transpose(0, 2, 4, 1, 3, 5, 6)
    return grid.reshape(extent_x * extent_y * extent_z // 8, 8 * channels)


def from_tokens(matrix, extent_x, extent_y, extent_z):
    channels = matrix.shape[1] // 8
    grid = matrix.reshape(extent_x // 2, extent_y // 2, extent_z // 2, 2, 2, 2, channels)
    grid = grid.transpose(0, 3, 1, 4, 2, 5, 6)
    return grid.reshape(extent_x, extent_y, extent_z, channels)


def gather_patches(padded, extent_x, extent_y, extent_z, flipped):
    channels = padded.shape[3]
    pieces = []
    for offset_x in range(3):
        for offset_y in range(3):
            for offset_z in range(3):
                start_x = 2 - offset_x if flipped else offset_x
                start_y = 2 - offset_y if flipped else offset_y
                start_z = 2 - offset_z if flipped else offset_z
                pieces.append(
                    padded[
                        start_x : start_x + extent_x,
                        start_y : start_y + extent_y,
                        start_z : start_z + extent_z,
                    ]
                )
    joined = jnp.concatenate(pieces, axis=3)
    return joined.reshape(extent_x * extent_y * extent_z, 27 * channels)


def local(features, conv_weight, down_weight, norm_gain, qkv_weight, out_weight, upstream):
    extent_x, extent_y, extent_z, channels = features.shape
    model_width = out_weight.shape[0]
    voxels = extent_x * extent_y * extent_z
    score_scale = HD ** (-0.5)
    padded = padded_2(features, (("gx", 0), ("gy", 1)), 1)
    padded = jnp.pad(padded, ((0, 0), (0, 0), (1, 1), (0, 0)))
    patches = gather_patches(padded, extent_x, extent_y, extent_z, False)
    hidden = jnp.dot(patches, conv_weight, preferred_element_type=jnp.float32)
    gate_sig = jax.nn.sigmoid(hidden)
    activation = (hidden * gate_sig).astype(jnp.bfloat16)
    tokens_in = to_tokens(activation.reshape(extent_x, extent_y, extent_z, channels))
    tok_count = tokens_in.shape[0]
    trunk_rows = jnp.dot(tokens_in, down_weight, preferred_element_type=jnp.float32)
    mean_rows = jnp.mean(trunk_rows, axis=-1, keepdims=True)
    centred = trunk_rows - mean_rows
    inverse_std = lax.rsqrt(jnp.mean(centred * centred, axis=-1, keepdims=True) + 1e-05)
    normed = centred * inverse_std
    normed_b = (normed * norm_gain).astype(jnp.bfloat16)
    qkv_rows = jnp.dot(normed_b, qkv_weight, preferred_element_type=jnp.float32).astype(
        jnp.bfloat16
    )
    queries = qkv_rows[:, :model_width]
    local_keys = qkv_rows[:, model_width : 2 * model_width]
    local_values = qkv_rows[:, 2 * model_width :]
    all_keys, all_values = (
        lax.all_gather(local_keys, ("gx", "gy"), axis=0, tiled=True),
        lax.all_gather(local_values, ("gx", "gy"), axis=0, tiled=True),
    )
    queries_h = queries.reshape(tok_count, H, HD)
    keys_h = all_keys.reshape(-1, H, HD)
    values_h = all_values.reshape(-1, H, HD)
    scores = (
        jnp.einsum("ihe,jhe->hij", queries_h, keys_h, preferred_element_type=jnp.float32)
        * score_scale
    )
    exp_scores = jnp.exp(scores)
    totals = jnp.sum(exp_scores, axis=-1)
    attn_probs = exp_scores / totals[:, :, None]
    probs_b = attn_probs.astype(jnp.bfloat16)
    attended = jnp.einsum("hij,jhe->ihe", probs_b, values_h, preferred_element_type=jnp.float32)
    attended = attended.reshape(tok_count, model_width).astype(jnp.bfloat16)
    cotangent = upstream.reshape(tok_count, model_width)
    cot_float = cotangent.astype(jnp.float32)
    out_part = jnp.einsum("td,te->de", attended, cotangent, preferred_element_type=jnp.float32)
    d_attended = jnp.dot(cotangent, out_weight.T, preferred_element_type=jnp.float32).astype(
        jnp.bfloat16
    )
    d_att_h = d_attended.reshape(tok_count, H, HD)
    d_probs = jnp.einsum("ihe,jhe->hij", d_att_h, values_h, preferred_element_type=jnp.float32)
    d_probs = d_probs.astype(jnp.bfloat16).astype(jnp.float32)
    row_delta = jnp.sum(attn_probs * d_probs, axis=-1)
    d_scores = attn_probs * (d_probs - row_delta[:, :, None])
    d_queries = (
        jnp.einsum(
            "hij,jhe->ihe", d_scores, keys_h, precision=precise, preferred_element_type=jnp.float32
        )
        * score_scale
    )
    key_term = (
        jnp.einsum(
            "hij,ihe->jhe",
            d_scores,
            queries_h,
            precision=precise,
            preferred_element_type=jnp.float32,
        )
        * score_scale
    )
    value_term = jnp.einsum("hij,ihe->jhe", probs_b, d_att_h, preferred_element_type=jnp.float32)
    key_sums = lax.psum_scatter(
        jnp.concatenate(
            [
                key_term.reshape(tok_count * lax.axis_size(("gx", "gy")), model_width),
                value_term.reshape(tok_count * lax.axis_size(("gx", "gy")), model_width),
            ],
            axis=1,
        ).astype(jnp.bfloat16),
        ("gx", "gy"),
        scatter_dimension=0,
        tiled=True,
    ).astype(jnp.float32)
    d_keys = key_sums[:, :model_width].astype(jnp.bfloat16)
    d_values = key_sums[:, model_width:].astype(jnp.bfloat16)
    d_qkv = jnp.concatenate(
        [d_queries.reshape(tok_count, model_width).astype(jnp.bfloat16), d_keys, d_values], axis=1
    )
    qkv_part = jnp.einsum("td,te->de", normed_b, d_qkv, preferred_element_type=jnp.float32)
    d_normed = (
        jnp.dot(d_qkv, qkv_weight.T, preferred_element_type=jnp.float32)
        .astype(jnp.bfloat16)
        .astype(jnp.float32)
    )
    d_hat = d_normed * norm_gain
    gain_part = jnp.sum(d_normed * normed, axis=0)
    gain_sum = lax.psum_scatter(gain_part, ("gx", "gy"), scatter_dimension=0, tiled=True)
    d_trunk = cot_float + inverse_std * (
        d_hat
        - jnp.mean(d_hat, axis=-1, keepdims=True)
        - normed * jnp.mean(d_hat * normed, axis=-1, keepdims=True)
    )
    down_part = jnp.einsum(
        "tr,td->rd", tokens_in, d_trunk, precision=precise, preferred_element_type=jnp.float32
    )
    d_activation = jnp.dot(
        d_trunk, down_weight.T, precision=precise, preferred_element_type=jnp.float32
    ).astype(jnp.bfloat16)
    d_act_grid = (
        from_tokens(d_activation, extent_x, extent_y, extent_z)
        .reshape(voxels, channels)
        .astype(jnp.float32)
    )
    d_hidden = (d_act_grid * gate_sig * (1.0 + hidden * (1.0 - gate_sig))).astype(jnp.bfloat16)
    conv_part = jnp.einsum("vr,vc->rc", patches, d_hidden, preferred_element_type=jnp.float32)
    d_padded = padded_2(
        d_hidden.reshape(extent_x, extent_y, extent_z, channels), (("gx", 0), ("gy", 1)), 1
    )
    d_padded = jnp.pad(d_padded, ((0, 0), (0, 0), (1, 1), (0, 0)))
    d_patches = gather_patches(d_padded, extent_x, extent_y, extent_z, True)
    conv_flip = (
        conv_weight.reshape(27, channels, channels)
        .transpose(0, 2, 1)
        .reshape(27 * channels, channels)
    )
    grad_features = jnp.dot(d_patches, conv_flip, preferred_element_type=jnp.float32)
    grad_features = grad_features.reshape(extent_x, extent_y, extent_z, channels).astype(
        jnp.bfloat16
    )
    conv_sum, down_sum, qkv_sum, out_sum = (
        lax.psum_scatter(
            conv_part.astype(jnp.bfloat16), ("gx", "gy"), scatter_dimension=0, tiled=True
        ).astype(jnp.float32),
        lax.psum_scatter(
            down_part.astype(jnp.bfloat16), ("gx", "gy"), scatter_dimension=0, tiled=True
        ).astype(jnp.float32),
        lax.psum_scatter(
            qkv_part.astype(jnp.bfloat16), ("gx", "gy"), scatter_dimension=0, tiled=True
        ).astype(jnp.float32),
        lax.psum_scatter(
            out_part.astype(jnp.bfloat16), ("gx", "gy"), scatter_dimension=0, tiled=True
        ).astype(jnp.float32),
    )
    return (
        grad_features,
        conv_sum.astype(jnp.bfloat16),
        down_sum.astype(jnp.bfloat16),
        gain_sum,
        qkv_sum.astype(jnp.bfloat16),
        out_sum.astype(jnp.bfloat16),
    )


def solution(mesh):
    placed = (
        P(("batch", "gx"), "gy", None, None),
        P(),
        P(),
        P(),
        P(),
        P(),
        P(("batch", "gx"), "gy", None, None),
    )
    return jax.shard_map(
        local,
        mesh=mesh,
        in_specs=placed,
        out_specs=(
            P(("batch", "gx"), "gy", None, None),
            P(("batch", "gx", "gy"), None),
            P(("batch", "gx", "gy"), None),
            P(("batch", "gx", "gy")),
            P(("batch", "gx", "gy"), None),
            P(("batch", "gx", "gy"), None),
        ),
        check_vma=False,
    )
```

profile of v0, /device:TPU:16, one launch (start us, length us, event | category | flops | bytes accessed | tf_op | source)
XLA Modules:
  0.0 585.7 jit_solution(17432155267392307056)
XLA Ops:
  14.1 3.4 collective-permute-start.2
  19.2 4.2 collective-permute-done.3
  28.6 2.1 fusion.61
  55.8 22.7 %reshape.89 = bf16[1024,6912]{1,0:T(8,128)(2,1)} reshape(bf16[16,16,4,6912]{3,2,1,0:T(4,128)(2,1)} %slice_dynamic-update-slice_fusion.18) | data formatting | bytes 28311552 | tf_op jit(solution)/shard_map/reshape | solution.py:55
  78.6 10.9 %multiply_convert_fusion.2 = (bf16[1024,256]{1,0:T(8,128)(2,1)S(1)}, f32[1024,256]{1,0:T(8,128)}) fusion(bf16[1024,6912]{1,0:T(8,128)(2,1)} %reshape.89, bf16[6912,256]{1,0:T(8,128)(2,1)} %param.8), kind=kOutput, calls=%fused_computation.54 | convolution fusion | flops 3625189376 | bytes 19267584 | tf_op jit(solution)/shard_map/dot_general | solution.py:66
  97.2 49.0 %all-gather.3.cloned.1.call-done = bf16[2048,512]{1,0:T(8,128)(2,1)} async-done(((bf16[128,512]{1,0:T(8,128)(2,1)}), bf16[2048,512]{1,0:T(8,128)(2,1)}) %all-gather.3.cloned.1.call-update) | async-done | bytes 2097168 | tf_op jit(solution)/shard_map/all_gather | solution.py:84
  146.2 4.1 copy.45
  150.3 3.1 fusion.3
  153.4 3.3 copy-done.2
  156.7 3.0 convolution_convert_fusion.4
  159.7 39.5 %all-gather.5.cloned.1.call-done = bf16[2048,512]{1,0:T(8,128)(2,1)} async-done(((bf16[128,512]{1,0:T(8,128)(2,1)}), bf16[2048,512]{1,0:T(8,128)(2,1)}) %all-gather.5.cloned.1.call-update) | async-done | bytes 2097168 | tf_op jit(solution)/shard_map/all_gather | solution.py:85
  199.2 4.0 copy.48
  203.1 6.7 %fusion = (f32[8,128]{1,0:T(8,128)S(1)}, bf16[8,128,2048]{2,1,0:T(8,128)(2,1)S(1)}) fusion(f32[8,128]{1,0:T(8,128)S(1)} %get-tuple-element.44, f32[8,128,2048]{2,1,0:T(8,128)} %copy-done.2, bf16[128,8,64]{0,2,1:T(8,128)(2,1)S(1)} %bitcast.71, bf16[2048,8,64]{0,2,1:T(8,128)(2,1)} %bitcast.61), kind=kOutput, calls=%fused_computation.3 | convolution fusion | flops 281017344 | bytes 14819328 | tf_op jit(solution)/shard_map/ihe,jhe->hij/dot_general | solution.py:107
  209.9 5.9 %multiply_convert_fusion = bf16[8,64,2048]{2,1,0:T(8,128)(2,1)S(1)} fusion(bf16[128,8,64]{0,2,1:T(8,128)(2,1)S(1)} %bitcast.67, bf16[8,128,2048]{2,1,0:T(8,128)(2,1)S(1)} %get-tuple-element.47, f32[8,128]{1,0:T(8,128)S(1)} %get-tuple-element.46, f32[8,128,2048]{2,1,0:T(8,128)S(1)} %copy-done.3, f32[8,128]{1,0:T(8,128)S(1)} %get-tuple-element.44), kind=kOutput, calls=%fused_computation.11 | convolution fusion | flops 1623195648 | bytes 14819328 | tf_op jit(solution)/shard_map/hij,ihe->jhe/dot_general | solution.py:118
  215.8 2.5 pad_maximum_fusion
  218.3 6.4 %copy.59 = bf16[2048,1024]{1,0:T(8,128)(2,1)} copy(bf16[2048,1024]{0,1:T(8,128)(2,1)} %pad_maximum_fusion) | data formatting | bytes 8388608
  224.8 5.7 fusion.31
  231.9 11.9 %fusion.34 = bf16[8,64,128]{2,1,0:T(8,128)(2,1)S(1)} fusion(bf16[2048,8,64]{0,2,1:T(8,128)(2,1)} %bitcast.57, bf16[8,128,2048]{2,1,0:T(8,128)(2,1)} %copy-done.14, f32[8,128]{1,0:T(8,128)S(1)} %get-tuple-element.46, f32[8,128,2048]{2,1,0:T(8,128)} %copy-done.2, f32[8,128]{1,0:T(8,128)S(1)} %get-tuple-element.44), kind=kOutput, calls=%fused_computation.49 | convolution fusion | flops 1621229568 | bytes 14819328 | tf_op jit(solution)/shard_map/hij,jhe->ihe/dot_general | solution.py:112
  243.8 56.7 %reduce-scatter.16.cloned.1.call-done = bf16[128,1024]{1,0:T(8,128)(2,1)} async-done(((bf16[2048,1024]{1,0:T(8,128)(2,1)}), bf16[128,1024]{1,0:T(8,128)(2,1)}) %reduce-scatter.16.cloned.1.call-update) | async-done | bytes 262160
  303.6 2.8 multiply_reduce_fusion
  306.4 3.3 convolution_convert_fusion.2
  310.2 3.1 fusion.14
  315.3 2.7 copy.66
  318.0 1.9 reshape.100
  323.6 5.7 copy.56
  330.6 2.0 reshape.97
  340.4 10.7 %convolution_convert_fusion = bf16[6912,256]{1,0:T(8,128)(2,1)} fusion(bf16[1024,6912]{1,0:T(8,128)(2,1)} %reshape.89, bf16[1024,256]{1,0:T(8,128)(2,1)} %copy-done.6), kind=kOutput, calls=%fused_computation.2 | convolution fusion | flops 3625648128 | bytes 18219008 | tf_op jit(solution)/shard_map/vr,vc->rc/dot_general | solution.py:171
  351.2 30.0 %all-reduce.2 = f32[512]{0:T(512)S(1)} all-reduce(f32[512]{0:T(512)S(1)} %copy-done.12), channel_id=5, replica_groups=mesh['batch'=16,'gx'=4,'gy'=4] {'gx','gy'}, use_global_device_ids=true, to_apply=%region_10.11.clone | all-reduce | flops 512 | bytes 4096
  387.1 3.8 convolution_convert_fusion.7
  392.0 42.7 %reduce-scatter.12.cloned.1.call-done = bf16[32,1536]{1,0:T(8,128)(2,1)} async-done(((bf16[512,1536]{1,0:T(8,128)(2,1)}), bf16[32,1536]{1,0:T(8,128)(2,1)}) %reduce-scatter.12.cloned.1.call-update) | async-done | bytes 98320 | tf_op jit(solution)/shard_map/reduce_scatter | solution.py:193
  434.7 69.8 %reduce-scatter.10.cloned.1.call-done = bf16[128,512]{1,0:T(8,128)(2,1)} async-done(((bf16[2048,512]{1,0:T(8,128)(2,1)}), bf16[128,512]{1,0:T(8,128)(2,1)}) %reduce-scatter.10.cloned.1.call-update) | async-done | bytes 131088 | tf_op jit(solution)/shard_map/reduce_scatter | solution.py:190
  504.5 74.1 %reduce-scatter.8.cloned.1.call-done = bf16[432,256]{1,0:T(8,128)(2,1)} async-done(((bf16[6912,256]{1,0:T(8,128)(2,1)}), bf16[432,256]{1,0:T(8,128)(2,1)}) %reduce-scatter.8.cloned.1.call-update) | async-done | bytes 221200 | tf_op jit(solution)/shard_map/reduce_scatter | solution.py:187
  (149 shorter events, 72.0 us)
Async XLA Ops:
  7.2 83.3 %copy-start = (bf16[2048,512]{1,0:T(8,128)(2,1)S(1)}, bf16[2048,512]{1,0:T(8,128)(2,1)}, u32[]{:S(2)}) copy-start(bf16[2048,512]{1,0:T(8,128)(2,1)} %param.9) | copy-start | bytes 6291460
  7.2 139.0 %all-gather.3.cloned.1.call-start = ((), (), s32[]{:S(2)}) async-start(), calls=%async_computation.5 | async-start | bytes 2228224 | tf_op jit(solution)/shard_map/all_gather | solution.py:84
  8.2 3.1 collective-permute-start
  9.9 4.2 collective-permute-start.1
  11.2 28.6 %copy-start.1 = (bf16[16,16,4,256]{3,2,1,0:T(4,128)(2,1)S(1)}, bf16[16,16,4,256]{3,2,1,0:T(4,128)(2,1)}, u32[]{:S(2)}) copy-start(bf16[16,16,4,256]{3,2,1,0:T(4,128)(2,1)} %param.7) | copy-start | bytes 1572868
  14.1 5.0 collective-permute-start.2
  17.6 5.9 collective-permute-start.3
  78.6 12.6 %copy-start.10 = (f32[512]{0:T(512)S(1)}, f32[512]{0:T(512)}, u32[]{:S(2)}) copy-start(f32[512]{0:T(512)} %param.10) | copy-start | bytes 6148
  93.8 105.4 %all-gather.5.cloned.1.call-start = ((), (), s32[]{:S(2)}) async-start(), calls=%async_computation.6 | async-start | bytes 2228224 | tf_op jit(solution)/shard_map/all_gather | solution.py:85
  94.5 206.1 %reduce-scatter.16.cloned.1.call-start = ((), (), s32[]{:S(2)}) async-start(), calls=%async_computation.11 | async-start | bytes 4456448
  153.4 3.3 copy-start.2
  203.1 6.8 %copy-start.3 = (f32[8,128,2048]{2,1,0:T(8,128)S(1)}, f32[8,128,2048]{2,1,0:T(8,128)}, u32[]{:S(2)}) copy-start(f32[8,128,2048]{2,1,0:T(8,128)} %copy-done.2) | copy-start | bytes 25165828
  209.9 5.9 %copy-start.14 = (bf16[8,128,2048]{2,1,0:T(8,128)(2,1)}, bf16[8,128,2048]{2,1,0:T(8,128)(2,1)S(1)}, u32[]{:S(2)}) copy-start(bf16[8,128,2048]{2,1,0:T(8,128)(2,1)S(1)} %get-tuple-element.47) | copy-start | bytes 12582916
  209.9 5.9 %copy-start.7 = (bf16[8,64,2048]{2,1,0:T(8,128)(2,1)S(1)}, bf16[8,64,2048]{2,1,0:T(8,128)(2,1)}, u32[]{:S(2)}) copy-start(bf16[8,64,2048]{2,1,0:T(8,128)(2,1)} %convolution_convert_fusion.4) | copy-start | bytes 6291460
  224.8 167.3 %reduce-scatter.14.cloned.1.call-start = ((), (), s32[]{:S(2)}) async-start(), calls=%async_computation.10 | async-start | bytes 557056 | tf_op jit(solution)/shard_map/reduce_scatter | solution.py:196
  231.7 203.1 %reduce-scatter.12.cloned.1.call-start = ((), (), s32[]{:S(2)}) async-start(), calls=%async_computation.9 | async-start | bytes 1671168 | tf_op jit(solution)/shard_map/reduce_scatter | solution.py:193
  243.8 59.7 %copy-start.9 = (bf16[8,64,128]{2,1,0:T(8,128)(2,1)}, bf16[8,64,128]{2,1,0:T(8,128)(2,1)S(1)}, u32[]{:S(2)}) copy-start(bf16[8,64,128]{2,1,0:T(8,128)(2,1)S(1)} %fusion.34) | copy-start | bytes 393220
  303.6 201.0 %reduce-scatter.10.cloned.1.call-start = ((), (), s32[]{:S(2)}) async-start(), calls=%async_computation.8 | async-start | bytes 2228224 | tf_op jit(solution)/shard_map/reduce_scatter | solution.py:190
  306.4 3.4 copy-start.8
  306.4 3.4 copy-start.11
  309.8 268.8 %reduce-scatter.8.cloned.1.call-start = ((), (), s32[]{:S(2)}) async-start(), calls=%async_computation.7 | async-start | bytes 3760128 | tf_op jit(solution)/shard_map/reduce_scatter | solution.py:187
  313.4 16.0 %copy-start.13 = (u32[256]{0:T(256)S(1)}, u32[256]{0:T(256)}, u32[]{:S(2)}) copy-start(u32[256]{0:T(256)} %constant.27) | copy-start | bytes 3076
  321.5 0.8 copy-start.6
  322.3 11.6 %collective-permute-start.4 = (bf16[1,16,4,256]{3,1,2,0:T(8,128)(2,1)S(1)}, bf16[1,16,4,256]{3,1,2,0:T(8,128)(2,1)S(1)}, u32[]{:S(2)}, u32[]{:S(2)}) collective-permute-start(bf16[1,16,4,256]{3,1,2,0:T(8,128)(2,1)S(1)} %copy.50), channel_id=1, source_target_pairs={{0,4},{4,8},{8,12},{1,5},{5,9},{9,13},{2,6},{6,10},{10,14},{3,7},{... | collective-permute-start | bytes 98312 | tf_op jit(solution)/shard_map/ppermute | solution.py:16
  332.7 4.4 collective-permute-start.5
  337.8 44.0 %collective-permute-start.6 = (bf16[18,1,4,256]{3,1,2,0:T(2,128)(2,1)}, bf16[18,1,4,256]{3,1,2,0:T(2,128)(2,1)S(1)}, u32[]{:S(2)}, u32[]{:S(2)}) collective-permute-start(bf16[18,1,4,256]{3,1,2,0:T(2,128)(2,1)} %get-tuple-element.27), channel_id=1, source_target_pairs={{0,1},{1,2},{2,3},{4,5},{5,6},{6,7},{8,9},{9,10},{10,11},{12,13},{... | collective-permute-start | bytes 110600 | tf_op jit(solution)/shard_map/ppermute | solution.py:16
  339.1 12.1 %copy-start.12 = (f32[512]{0:T(512)S(1)}, f32[512]{0:T(512)}, u32[]{:S(2)}) copy-start(f32[512]{0:T(512)} %get-tuple-element.24) | copy-start | bytes 6148
  339.1 42.7 %collective-permute-start.7 = (bf16[18,1,4,256]{3,1,2,0:T(2,128)(2,1)S(1)}, bf16[18,1,4,256]{3,1,2,0:T(2,128)(2,1)S(1)}, u32[]{:S(2)}, u32[]{:S(2)}) collective-permute-start(bf16[18,1,4,256]{3,1,2,0:T(2,128)(2,1)S(1)} %get-tuple-element.28), channel_id=1, source_target_pairs={{1,0},{2,1},{3,2},{5,4},{6,5},{7,6},{9,8},{10,9},{11,10},{13,12},{... | collective-permute-start | bytes 110600 | tf_op jit(solution)/shard_map/ppermute | solution.py:19
  381.2 3.7 copy-start.4
  384.5 2.6 copy-start.5
Sparse Core Ops, SparseCore 0:
  93.9 52.2 all-gather.2
  148.6 50.5 all-gather.4
  224.9 75.6 reduce-scatter.15
  303.5 62.8 reduce-scatter.13
  369.4 65.2 reduce-scatter.11
  437.7 66.8 reduce-scatter.9
  507.7 70.9 reduce-scatter.7
where the time goes:
time: 593 us; the launch traced here: 586 us
  waiting for transfers between devices  341 us (58%)
  local copies, waits for them, and re-layouts  90.4 us (15%)
  matrix products  77.6 us (13%)
  blocking collectives  30 us (5%)
  other arithmetic  17.6 us (3%)
  between operations  15.6 us (3%)
  starting transfers between devices  13.8 us (2%)
    reduce_scatter x1, waiting for transfers between devices, local(): lax.psum_scatter(conv_part.astype(jnp.bfloat16), ('gx', 'gy'), scatter_di...  74.1 us
    reduce_scatter x1, waiting for transfers between devices, local(): lax.psum_scatter(down_part.astype(jnp.bfloat16), ('gx', 'gy'), scatter_di...  69.8 us
    unnamed x8, waiting for transfers between devices  57.5 us
    all_gather x1, waiting for transfers between devices, local(): lax.all_gather(local_keys, ('gx', 'gy'), axis=0, tiled=True)  49 us
    reduce_scatter x1, waiting for transfers between devices, local(): lax.psum_scatter(qkv_part.astype(jnp.bfloat16), ('gx', 'gy'), scatter_dim...  42.7 us
    all_gather x1, waiting for transfers between devices, local(): lax.all_gather(local_values, ('gx', 'gy'), axis=0, tiled=True)  39.5 us
    unnamed x74, local copies, waits for them, and re-layouts  38.3 us
    unnamed x1, blocking collectives  30 us
  transfers between devices with their start and end apart: 15, of which 10 were waited for; matrix products, arithmetic and copies ran while one was open for 14% of the time, Pallas kernels for 0%

commit v1 on v0

--- a/solution.py
+++ b/solution.py
@@ -6,6 +6,18 @@
 H = 8
 HD = 64
 precise = lax.Precision.HIGHEST
+
+
+def columns_place(xs):
+    return jnp.concatenate(
+        lax.all_to_all(
+            jnp.stack(tuple((xs for _ in range(lax.axis_size(("gx", "gy"))))), axis=0),
+            ("gx", "gy"),
+            split_axis=0,
+            concat_axis=0,
+        ),
+        0,
+    )
 
 
 def padded_2(block, sides, width):
@@ -82,7 +94,7 @@
     local_values = qkv_rows[:, 2 * model_width :]
     all_keys, all_values = (
         lax.all_gather(local_keys, ("gx", "gy"), axis=0, tiled=True),
-        lax.all_gather(local_values, ("gx", "gy"), axis=0, tiled=True),
+        columns_place(local_values),
     )
     queries_h = queries.reshape(tok_count, H, HD)
     keys_h = all_keys.reshape(-1, H, HD)

time: 593 us -> 556 us (0.938)
  waiting for transfers between devices: 341 us -> 297 us
    all_gather x1 -> x0, waiting for transfers between devices: 39.5 us -> none  [local(): lax.all_gather(local_values, ('gx', 'gy'), axis=0, tiled=True)]
    all_gather x1, waiting for transfers between devices: 49 us -> 16.3 us  [local(): lax.all_gather(local_keys, ('gx', 'gy'), axis=0, tiled=True)]
    all_to_all x0 -> x1, waiting for transfers between devices: none -> 28.7 us  [columns_place(): lax.all_to_all(jnp.stack(tuple((xs for _ in range(lax.axis_size(('gx', 'g...]
    all_to_all x0 -> x1, starting transfers between devices: none -> 6.12 us  [columns_place(): lax.all_to_all(jnp.stack(tuple((xs for _ in range(lax.axis_size(('gx', 'g...]
    another operation x0 -> x2, local copies, waits for them, and re-layouts: none -> 6.05 us  [the longest x1 4.31 us: local(): values_h = all_values.reshape(-1, H, HD)]
    unnamed x74 -> x72, local copies, waits for them, and re-layouts: 38.3 us -> 36 us
    unnamed x8 -> x7, waiting for transfers between devices: 57.5 us -> 58.4 us
  transfers between devices with their start and end apart: 15 -> 15, of which waited for: 10 -> 10; matrix products, arithmetic and copies ran while one was open for 14% -> 16% of each run, Pallas kernels for 0% -> 0%
where the time goes in v1:
time: 556 us; the launch traced here: 548 us
  waiting for transfers between devices  297 us (53%)
  local copies, waits for them, and re-layouts  94.4 us (17%)
  matrix products  72.6 us (13%)
  blocking collectives  30.3 us (5%)
  starting transfers between devices  19.7 us (4%)
  other arithmetic  17.8 us (3%)
  between operations  15.9 us (3%)
    reduce_scatter x1, waiting for transfers between devices, local(): lax.psum_scatter(conv_part.astype(jnp.bfloat16), ('gx', 'gy'), scatter_di...  74.3 us
    reduce_scatter x1, waiting for transfers between devices, local(): lax.psum_scatter(down_part.astype(jnp.bfloat16), ('gx', 'gy'), scatter_di...  69.4 us
    unnamed x7, waiting for transfers between devices  58.4 us
    reduce_scatter x1, waiting for transfers between devices, local(): lax.psum_scatter(qkv_part.astype(jnp.bfloat16), ('gx', 'gy'), scatter_dim...  42.7 us
    unnamed x72, local copies, waits for them, and re-layouts  36 us
    unnamed x1, blocking collectives  30.3 us
    all_to_all x1, waiting for transfers between devices, columns_place(): lax.all_to_all(jnp.stack(tuple((xs for _ in range(lax.axis_size(('gx', 'g...  28.7 us
    reshape x1, local copies, waits for them, and re-layouts, gather_patches(): return joined.reshape(extent_x * extent_y * extent_z, 27 * channels)  22.7 us
  transfers between devices with their start and end apart: 15, of which 10 were waited for; matrix products, arithmetic and copies ran while one was open for 16% of the time, Pallas kernels for 0%

profile of v1, /device:TPU:16, one launch (start us, length us, event | category | flops | bytes accessed | tf_op | source)
XLA Modules:
  0.0 548.1 jit_solution(16050231064842160327)
XLA Ops:
  14.1 3.4 collective-permute-start.2
  19.2 4.2 collective-permute-done.3
  28.6 2.2 fusion.61
  55.9 22.7 %reshape.88 = bf16[1024,6912]{1,0:T(8,128)(2,1)} reshape(bf16[16,16,4,6912]{3,2,1,0:T(4,128)(2,1)} %slice_dynamic-update-slice_fusion.18) | data formatting | bytes 28311552 | tf_op jit(solution)/shard_map/reshape | solution.py:67
  78.6 10.9 %multiply_convert_fusion.2 = (bf16[1024,256]{1,0:T(8,128)(2,1)S(1)}, f32[1024,256]{1,0:T(8,128)}) fusion(bf16[1024,6912]{1,0:T(8,128)(2,1)} %reshape.88, bf16[6912,256]{1,0:T(8,128)(2,1)} %param.8), kind=kOutput, calls=%fused_computation.54 | convolution fusion | flops 3625189376 | bytes 19267584 | tf_op jit(solution)/shard_map/dot_general | solution.py:78
  95.6 6.1 %all-to-all-start = ((bf16[16,128,512]{1,2,0:T(8,128)(2,1)}), bf16[16,128,512]{1,2,0:T(8,128)(2,1)}, u32[]{:S(2)}, u32[]{:S(2)}) async-start(bf16[16,128,512]{1,2,0:T(8,128)(2,1)} %stack.2), calls=%async_computation | async-start | bytes 4194304 | tf_op jit(solution)/shard_map/all_to_all | solution.py:13
  104.4 28.7 %all-to-all-done = bf16[16,128,512]{1,2,0:T(8,128)(2,1)} async-done(((bf16[16,128,512]{1,2,0:T(8,128)(2,1)}), bf16[16,128,512]{1,2,0:T(8,128)(2,1)}, u32[]{:S(2)}, u32[]{:S(2)}) %all-to-all-start) | async-done | bytes 2097184 | tf_op jit(solution)/shard_map/all_to_all | solution.py:13
  133.1 4.3 copy.48
  137.4 4.3 reshape_reshape.8
  141.7 16.3 %all-gather.2.cloned.1.call-done = bf16[2048,512]{1,0:T(8,128)(2,1)} async-done(((bf16[128,512]{1,0:T(8,128)(2,1)}), bf16[2048,512]{1,0:T(8,128)(2,1)}) %all-gather.2.cloned.1.call-update) | async-done | bytes 2097168 | tf_op jit(solution)/shard_map/all_gather | solution.py:96
  158.0 3.9 copy.44
  162.0 3.1 fusion.3
  165.1 2.0 convolution_convert_fusion.4
  168.2 2.7 fusion
  171.0 5.9 %multiply_convert_fusion = bf16[8,64,2048]{2,1,0:T(8,128)(2,1)S(1)} fusion(bf16[128,8,64]{0,2,1:T(8,128)(2,1)S(1)} %bitcast.66, bf16[8,128,2048]{2,1,0:T(8,128)(2,1)S(1)} %get-tuple-element.47, f32[8,128]{1,0:T(8,128)S(1)} %get-tuple-element.46, f32[8,128,2048]{2,1,0:T(8,128)S(1)} %get-tuple-element.45, f32[8,128]{1,0:T(8,128)S(1)} %get-tuple-element.44), kind=kOutput, calls=%fused_computation.11 | convolution fusion | flops 1623195648 | bytes 14819328 | tf_op jit(solution)/shard_map/hij,ihe->jhe/dot_general | solution.py:130
  176.8 2.5 pad_maximum_fusion
  179.4 6.4 %copy.59 = bf16[2048,1024]{1,0:T(8,128)(2,1)} copy(bf16[2048,1024]{0,1:T(8,128)(2,1)} %pad_maximum_fusion) | data formatting | bytes 8388608
  185.8 5.7 %fusion.31 = bf16[8,64,128]{2,1,0:T(8,128)(2,1)S(1)} fusion(bf16[2048,8,64]{0,2,1:T(8,128)(2,1)} %reshape_reshape.8, f32[8,128,2048]{2,1,0:T(8,128)} %copy-done.2, f32[8,128]{1,0:T(8,128)S(1)} %get-tuple-element.44), kind=kOutput, calls=%fused_computation.47 | convolution fusion | flops 274792448 | bytes 10620928 | tf_op jit(solution)/shard_map/hij,jhe->ihe/dot_general | solution.py:110
  193.0 11.9 %fusion.34 = bf16[8,64,128]{2,1,0:T(8,128)(2,1)S(1)} fusion(bf16[2048,8,64]{0,2,1:T(8,128)(2,1)} %bitcast.58, bf16[8,128,2048]{2,1,0:T(8,128)(2,1)} %copy-done.13, f32[8,128]{1,0:T(8,128)S(1)} %get-tuple-element.46, f32[8,128,2048]{2,1,0:T(8,128)} %copy-done.2, f32[8,128]{1,0:T(8,128)S(1)} %get-tuple-element.44), kind=kOutput, calls=%fused_computation.49 | convolution fusion | flops 1621229568 | bytes 14819328 | tf_op jit(solution)/shard_map/hij,jhe->ihe/dot_general | solution.py:124
  204.9 58.3 %reduce-scatter.16.cloned.1.call-done = bf16[128,1024]{1,0:T(8,128)(2,1)} async-done(((bf16[2048,1024]{1,0:T(8,128)(2,1)}), bf16[128,1024]{1,0:T(8,128)(2,1)}) %reduce-scatter.16.cloned.1.call-update) | async-done | bytes 262160
  266.2 2.8 multiply_reduce_fusion
  269.0 3.3 convolution_convert_fusion.2
  272.7 3.1 fusion.14
  277.7 2.7 copy.66
  286.1 5.7 %copy.56 = bf16[27,256,256]{2,1,0:T(8,128)(2,1)} copy(bf16[27,256,256]{1,2,0:T(8,128)(2,1)} %bitcast.60) | data formatting | bytes 7077888 | tf_op jit(solution)/shard_map/transpose | solution.py:191
  293.0 2.0 reshape.95
  302.5 10.8 %convolution_convert_fusion = bf16[6912,256]{1,0:T(8,128)(2,1)} fusion(bf16[1024,6912]{1,0:T(8,128)(2,1)} %reshape.88, bf16[1024,256]{1,0:T(8,128)(2,1)} %copy-done.5), kind=kOutput, calls=%fused_computation.2 | convolution fusion | flops 3625648128 | bytes 18219008 | tf_op jit(solution)/shard_map/vr,vc->rc/dot_general | solution.py:183
  313.3 30.3 %all-reduce.2 = f32[512]{0:T(512)S(1)} all-reduce(f32[512]{0:T(512)S(1)} %copy-done.11), channel_id=5, replica_groups=mesh['batch'=16,'gx'=4,'gy'=4] {'gx','gy'}, use_global_device_ids=true, to_apply=%region_10.11.clone | all-reduce | flops 512 | bytes 4096
  349.5 3.8 convolution_convert_fusion.7
  354.4 42.7 %reduce-scatter.12.cloned.1.call-done = bf16[32,1536]{1,0:T(8,128)(2,1)} async-done(((bf16[512,1536]{1,0:T(8,128)(2,1)}), bf16[32,1536]{1,0:T(8,128)(2,1)}) %reduce-scatter.12.cloned.1.call-update) | async-done | bytes 98320 | tf_op jit(solution)/shard_map/reduce_scatter | solution.py:205
  397.1 69.4 %reduce-scatter.10.cloned.1.call-done = bf16[128,512]{1,0:T(8,128)(2,1)} async-done(((bf16[2048,512]{1,0:T(8,128)(2,1)}), bf16[128,512]{1,0:T(8,128)(2,1)}) %reduce-scatter.10.cloned.1.call-update) | async-done | bytes 131088 | tf_op jit(solution)/shard_map/reduce_scatter | solution.py:202
  466.5 74.3 %reduce-scatter.8.cloned.1.call-done = bf16[432,256]{1,0:T(8,128)(2,1)} async-done(((bf16[6912,256]{1,0:T(8,128)(2,1)}), bf16[432,256]{1,0:T(8,128)(2,1)}) %reduce-scatter.8.cloned.1.call-update) | async-done | bytes 221200 | tf_op jit(solution)/shard_map/reduce_scatter | solution.py:199
  (149 shorter events, 75.6 us)
Async XLA Ops:
  7.2 83.3 %copy-start = (bf16[2048,512]{1,0:T(8,128)(2,1)S(1)}, bf16[2048,512]{1,0:T(8,128)(2,1)}, u32[]{:S(2)}) copy-start(bf16[2048,512]{1,0:T(8,128)(2,1)} %param.9) | copy-start | bytes 6291460
  7.2 150.8 %all-gather.2.cloned.1.call-start = ((), (), s32[]{:S(2)}) async-start(), calls=%async_computation.6 | async-start | bytes 2228224 | tf_op jit(solution)/shard_map/all_gather | solution.py:96
  8.2 3.1 collective-permute-start
  9.9 4.2 collective-permute-start.1
  11.2 28.7 %copy-start.1 = (bf16[16,16,4,256]{3,2,1,0:T(4,128)(2,1)S(1)}, bf16[16,16,4,256]{3,2,1,0:T(4,128)(2,1)}, u32[]{:S(2)}) copy-start(bf16[16,16,4,256]{3,2,1,0:T(4,128)(2,1)} %param.7) | copy-start | bytes 1572868
  14.1 5.0 collective-permute-start.2
  17.6 5.9 %collective-permute-start.3 = (bf16[18,1,4,256]{3,2,1,0:T(4,128)(2,1)S(1)}, bf16[18,1,4,256]{3,2,1,0:T(4,128)(2,1)S(1)}, u32[]{:S(2)}, u32[]{:S(2)}) collective-permute-start(bf16[18,1,4,256]{3,2,1,0:T(4,128)(2,1)S(1)} %get-tuple-element.30), channel_id=1, source_target_pairs={{1,0},{2,1},{3,2},{5,4},{6,5},{7,6},{9,8},{10,9},{11,10},{13,12},{... | collective-permute-start | bytes 110600 | tf_op jit(solution)/shard_map/ppermute | solution.py:31
  78.6 12.6 %copy-start.9 = (f32[512]{0:T(512)S(1)}, f32[512]{0:T(512)}, u32[]{:S(2)}) copy-start(f32[512]{0:T(512)} %param.10) | copy-start | bytes 6148
  95.6 37.5 %all-to-all-start = ((bf16[16,128,512]{1,2,0:T(8,128)(2,1)}), bf16[16,128,512]{1,2,0:T(8,128)(2,1)}, u32[]{:S(2)}, u32[]{:S(2)}) async-start(bf16[16,128,512]{1,2,0:T(8,128)(2,1)} %stack.2), calls=%async_computation | async-start | bytes 4194304 | tf_op jit(solution)/shard_map/all_to_all | solution.py:13
  101.7 161.4 %reduce-scatter.16.cloned.1.call-start = ((), (), s32[]{:S(2)}) async-start(), calls=%async_computation.11 | async-start | bytes 4456448
  165.1 5.9 %copy-start.2 = (f32[8,128,2048]{2,1,0:T(8,128)}, f32[8,128,2048]{2,1,0:T(8,128)S(1)}, u32[]{:S(2)}) copy-start(f32[8,128,2048]{2,1,0:T(8,128)S(1)} %get-tuple-element.45) | copy-start | bytes 25165828
  165.1 3.1 copy-start.6
  170.9 5.9 %copy-start.13 = (bf16[8,128,2048]{2,1,0:T(8,128)(2,1)}, bf16[8,128,2048]{2,1,0:T(8,128)(2,1)S(1)}, u32[]{:S(2)}) copy-start(bf16[8,128,2048]{2,1,0:T(8,128)(2,1)S(1)} %get-tuple-element.47) | copy-start | bytes 12582916
  185.8 168.6 %reduce-scatter.14.cloned.1.call-start = ((), (), s32[]{:S(2)}) async-start(), calls=%async_computation.10 | async-start | bytes 557056 | tf_op jit(solution)/shard_map/reduce_scatter | solution.py:208
  192.7 204.4 %reduce-scatter.12.cloned.1.call-start = ((), (), s32[]{:S(2)}) async-start(), calls=%async_computation.9 | async-start | bytes 1671168 | tf_op jit(solution)/shard_map/reduce_scatter | solution.py:205
  204.8 61.3 %copy-start.8 = (bf16[8,64,128]{2,1,0:T(8,128)(2,1)}, bf16[8,64,128]{2,1,0:T(8,128)(2,1)S(1)}, u32[]{:S(2)}) copy-start(bf16[8,64,128]{2,1,0:T(8,128)(2,1)S(1)} %fusion.34) | copy-start | bytes 393220
  266.1 200.4 %reduce-scatter.10.cloned.1.call-start = ((), (), s32[]{:S(2)}) async-start(), calls=%async_computation.8 | async-start | bytes 2228224 | tf_op jit(solution)/shard_map/reduce_scatter | solution.py:202
  269.0 3.4 copy-start.7
  269.0 3.4 copy-start.10
  272.4 268.4 %reduce-scatter.8.cloned.1.call-start = ((), (), s32[]{:S(2)}) async-start(), calls=%async_computation.7 | async-start | bytes 3760128 | tf_op jit(solution)/shard_map/reduce_scatter | solution.py:199
  275.8 16.0 %copy-start.12 = (u32[256]{0:T(256)S(1)}, u32[256]{0:T(256)}, u32[]{:S(2)}) copy-start(u32[256]{0:T(256)} %constant.27) | copy-start | bytes 3076
  283.9 0.8 copy-start.5
  284.8 11.6 %collective-permute-start.4 = (bf16[1,16,4,256]{3,1,2,0:T(8,128)(2,1)S(1)}, bf16[1,16,4,256]{3,1,2,0:T(8,128)(2,1)S(1)}, u32[]{:S(2)}, u32[]{:S(2)}) collective-permute-start(bf16[1,16,4,256]{3,1,2,0:T(8,128)(2,1)S(1)} %copy.50), channel_id=1, source_target_pairs={{0,4},{4,8},{8,12},{1,5},{5,9},{9,13},{2,6},{6,10},{10,14},{3,7},{... | collective-permute-start | bytes 98312 | tf_op jit(solution)/shard_map/ppermute | solution.py:28
  295.1 4.1 collective-permute-start.5
  299.9 44.2 %collective-permute-start.6 = (bf16[18,1,4,256]{3,1,2,0:T(2,128)(2,1)}, bf16[18,1,4,256]{3,1,2,0:T(2,128)(2,1)S(1)}, u32[]{:S(2)}, u32[]{:S(2)}) collective-permute-start(bf16[18,1,4,256]{3,1,2,0:T(2,128)(2,1)} %get-tuple-element.27), channel_id=1, source_target_pairs={{0,1},{1,2},{2,3},{4,5},{5,6},{6,7},{8,9},{9,10},{10,11},{12,13},{... | collective-permute-start | bytes 110600 | tf_op jit(solution)/shard_map/ppermute | solution.py:28
  301.2 12.1 %copy-start.11 = (f32[512]{0:T(512)S(1)}, f32[512]{0:T(512)}, u32[]{:S(2)}) copy-start(f32[512]{0:T(512)} %get-tuple-element.24) | copy-start | bytes 6148
  301.2 42.9 %collective-permute-start.7 = (bf16[18,1,4,256]{3,1,2,0:T(2,128)(2,1)S(1)}, bf16[18,1,4,256]{3,1,2,0:T(2,128)(2,1)S(1)}, u32[]{:S(2)}, u32[]{:S(2)}) collective-permute-start(bf16[18,1,4,256]{3,1,2,0:T(2,128)(2,1)S(1)} %get-tuple-element.28), channel_id=1, source_target_pairs={{1,0},{2,1},{3,2},{5,4},{6,5},{7,6},{9,8},{10,9},{11,10},{13,12},{... | collective-permute-start | bytes 110600 | tf_op jit(solution)/shard_map/ppermute | solution.py:31
  343.6 3.7 copy-start.3
  346.9 2.6 copy-start.4
Sparse Core Ops, SparseCore 0:
  93.9 64.0 all-gather.1
  185.9 77.1 reduce-scatter.15
  266.2 62.6 reduce-scatter.13
  331.8 65.2 reduce-scatter.11
  400.0 66.4 reduce-scatter.9
  469.5 71.2 reduce-scatter.7
